TPU v7x, 512 devices: a whole 4x4x16 slice. The times are simulated.
512 devices in a mesh: group: 32 (over y, z_lo, core), expert: 16 (over x, z_hi).
Axes of the slice: x: 4, y: 4, z: 16 (z_hi: 4, z_lo: 4; z = z_hi * 4 + z_lo), core: 2. Of those that a mesh axis runs over, the one named last changes fastest.
Arguments:
- tokens: bfloat16 [65536, 1536], P(('group', 'expert')), may hold values from -6 to 6
- gate_train: float32 [32, 1536, 512], P('expert', 'group'), may hold values from -0.15625 to 0.15625
- up_train: float32 [32, 1536, 512], P('expert', 'group'), may hold values from -0.15625 to 0.15625
- down_train: float32 [32, 512, 1536], P('expert', None, 'group'), may hold values from -0.25 to 0.25
- routes: int32 [65536, 6], P(('group', 'expert')), may hold values from 0 to 31, as said below
- route_scores: float32 [65536, 6], P(('group', 'expert')), may hold values from 0.05 to 1
- live: int32 [65536], P(('group', 'expert')), may hold values from 0 to 1
Outputs:
- moe_out: bfloat16 [65536, 1536], P(('group', 'expert'))
Inputs may be any that keep to these rules, and one draw needn't show every extreme that they name: `routes`: each row names 6 different experts; one expert, the same on every device, is named by at least 24 live rows among each device's 128 rows.
All inputs are finite; a program needn't handle non-finite values.
Results may differ from a plain program's by a relative error of at most 0.0075.
Values may be sent and summed in bfloat16 or wider, within the bound.
No kernel may reach another device: no remote copies, remote signals or barrier semaphores. Data moves between devices by JAX's collectives and lax.ppermute only.
A program may use at most 64 MiB of HBM per device.

v0:
```python
import jax
import jax.numpy as jnp
from jax import lax
from jax.sharding import PartitionSpec as P


def local(tokens, gate_train, up_train, down_train, routes, route_scores, live):
    local_experts = gate_train.shape[0]
    hidden_width = gate_train.shape[2]
    holders = lax.axis_size("expert")
    experts = local_experts * holders
    tok_dev, model_width = tokens.shape
    top_count = routes.shape[1]
    capacity = tok_dev * top_count // experts
    total_slots = experts * capacity
    route_share = route_scores / jnp.sum(route_scores, axis=1, keepdims=True)
    flat_route = routes.reshape(-1)
    flat_live = jnp.repeat(live, top_count)
    expert_ids = jnp.arange(experts, dtype=jnp.int32)
    onehot = ((flat_route[:, None] == expert_ids[None, :]) & (flat_live[:, None] > 0)).astype(
        jnp.int32
    )
    earlier = jnp.cumsum(onehot, axis=0) - onehot
    slot_index = jnp.sum(earlier * onehot, axis=1)
    kept_mask = (flat_live > 0) & (slot_index < capacity)
    target = jnp.where(kept_mask, flat_route * capacity + slot_index, total_slots)
    anchor = jnp.arange(tok_dev * top_count, dtype=jnp.int32) // top_count
    source_row = jnp.zeros((total_slots,), jnp.int32).at[target].set(anchor, mode="drop")
    filled = jnp.zeros((total_slots,), jnp.int32).at[target].set(1, mode="drop")
    outgoing = jnp.where(filled[:, None] > 0, tokens[source_row], jnp.zeros((), jnp.bfloat16))
    outgoing = outgoing.reshape(holders, local_experts * capacity, model_width)
    incoming = lax.all_to_all(outgoing, "expert", split_axis=0, concat_axis=0, tiled=True)
    incoming = incoming.reshape(holders, local_experts, capacity, model_width)
    gate_up_local = jnp.concatenate([gate_train, up_train], axis=2).astype(jnp.bfloat16)
    down_local = down_train.astype(jnp.bfloat16)
    gate_up_w, down_w = (
        lax.all_gather(gate_up_local, "group", axis=1, tiled=True),
        lax.all_gather(down_local, "group", axis=2, tiled=True),
    )
    gate_up = jnp.einsum("sjcd,jdf->sjcf", incoming, gate_up_w, preferred_element_type=jnp.float32)
    hidden = (jax.nn.silu(gate_up[..., :hidden_width]) * gate_up[..., hidden_width:]).astype(
        jnp.bfloat16
    )
    expert_out = jnp.einsum("sjcf,jfd->sjcd", hidden, down_w, preferred_element_type=jnp.float32)
    expert_rows = expert_out.astype(jnp.bfloat16).reshape(
        holders, local_experts * capacity, model_width
    )
    returned = lax.all_to_all(
        expert_rows, "expert", split_axis=0, concat_axis=0, tiled=True
    ).reshape(total_slots, model_width)
    picked = returned[jnp.minimum(target, total_slots - 1)]
    weight = jnp.where(kept_mask, route_share.reshape(-1), 0.0)
    combined = jnp.sum(
        picked.reshape(tok_dev, top_count, model_width).astype(jnp.float32)
        * weight.reshape(tok_dev, top_count, 1),
        axis=1,
    )
    return combined.astype(jnp.bfloat16)


def solution(mesh):
    in_specs = (
        P(("group", "expert"), None),
        P("expert", "group", None),
        P("expert", "group", None),
        P("expert", None, "group"),
        P(("group", "expert"), None),
        P(("group", "expert"), None),
        P(("group", "expert")),
    )
    out_specs = P(("group", "expert"), None)
    return jax.shard_map(local, mesh=mesh, in_specs=in_specs, out_specs=out_specs, check_vma=False)
```

profile of v0, /device:TPU:48, one launch (start us, length us, event | category | flops | bytes accessed | tf_op | source)
XLA Modules:
  0.0 405.2 jit_solution(16092670859250466878)
XLA Ops:
  6.5 0.0 copy-start
  6.5 0.0 all-gather.3.cloned.1.call-start
  6.5 1.0 convert.7
  7.5 0.9 convert.8
  8.5 0.7 pad_maximum_fusion
  9.2 0.0 all-gather.3.cloned.1.call-update
  9.2 0.7 broadcast_compare_fusion.2
  9.9 0.1 broadcast_in_dim.37.clone
  10.0 0.2 gt.41
  10.1 0.1 gt.40
  10.3 0.8 copy.18
  11.1 0.1 eq.29
  11.2 0.1 eq.25
  11.3 0.1 gt.39
  11.5 1.7 reduce-window.6
  13.2 0.3 slice_reduce_fusion
  13.5 0.7 broadcast_multiply_fusion
  14.2 0.1 copy.23
  14.3 0.1 mul.37
  14.5 0.1 fusion.17
  14.7 3.4 scatter_custom_fusion.1
  18.0 3.4 scatter_custom_fusion
  21.4 0.1 broadcast_in_dim.40
  21.6 0.0 copy-done
  21.6 2.9 gather_fusion
  24.5 1.6 broadcast_select_fusion
  26.1 0.0 copy-start.1
  26.1 16.9 %all-to-all-start = ((bf16[16,48,1536]{2,1,0:T(8,128)(2,1)}), bf16[16,48,1536]{2,1,0:T(8,128)(2,1)S(1)}, u32[]{:S(2)}, u32[]{:S(2)}) async-start(bf16[16,48,1536]{2,1,0:T(8,128)(2,1)} %broadcast_select_fusion), calls=%async_computation | async-start | bytes 4718592 | tf_op jit(solution)/shard_map/all_to_all | solution.py:32
  43.0 0.0 all-gather.5.cloned.1.call-start
  43.1 0.0 copy-done.1
  43.1 0.7 convert_element_type.32
  43.7 0.0 all-gather.5.cloned.1.call-update
  43.8 104.8 %all-to-all-done = bf16[16,48,1536]{2,1,0:T(8,128)(2,1)S(1)} async-done(((bf16[16,48,1536]{2,1,0:T(8,128)(2,1)}), bf16[16,48,1536]{2,1,0:T(8,128)(2,1)S(1)}, u32[]{:S(2)}, u32[]{:S(2)}) %all-to-all-start) | async-done | bytes 2359328 | tf_op jit(solution)/shard_map/all_to_all | solution.py:32
  148.6 32.2 %all-gather.3.cloned.1.call-done = bf16[2,1536,1024]{2,1,0:T(8,128)(2,1)} async-done(((bf16[2,48,1024]{2,1,0:T(8,128)(2,1)}), bf16[2,1536,1024]{2,1,0:T(8,128)(2,1)}) %all-gather.3.cloned.1.call-update) | async-done | bytes 6291472 | tf_op jit(solution)/shard_map/all_gather | solution.py:37
  180.8 7.0 %fusion.7 = f32[16,2,24,1024]{3,2,0,1:T(8,128)} fusion(bf16[16,2,24,1536]{3,2,1,0:T(8,128)(2,1)S(1)} %bitcast.45, bf16[2,1536,1024]{2,1,0:T(8,128)(2,1)} %all-gather.3.cloned.1.call-done), kind=kOutput, calls=%fused_computation.12 | convolution fusion | flops 2415919104 | bytes 11796480 | tf_op jit(solution)/shard_map/sjcd,jdf->sjcf/dot_general | solution.py:40
  187.9 62.0 %all-gather.5.cloned.1.call-done = bf16[2,512,1536]{1,2,0:T(8,128)(2,1)} async-done(((bf16[2,512,48]{1,2,0:T(8,128)(2,1)}), bf16[2,512,1536]{1,2,0:T(8,128)(2,1)}) %all-gather.5.cloned.1.call-update) | async-done | bytes 3145744 | tf_op jit(solution)/shard_map/all_gather | solution.py:38
  249.9 4.3 %fusion.3 = bf16[16,2,24,1536]{3,2,0,1:T(8,128)(2,1)S(1)} fusion(bf16[2,512,1536]{1,2,0:T(8,128)(2,1)} %all-gather.5.cloned.1.call-done, f32[16,2,24,1024]{3,2,0,1:T(8,128)} %fusion.7), kind=kOutput, calls=%fused_computation.9 | convolution fusion | flops 1211498496 | bytes 8650752 | tf_op jit(solution)/shard_map/sjcf,jfd->sjcd/dot_general | solution.py:44
  254.2 1.7 copy.25
  255.9 0.0 copy-start.2
  255.9 13.0 %all-to-all-start.1 = ((bf16[16,48,1536]{2,1,0:T(8,128)(2,1)}), bf16[16,48,1536]{2,1,0:T(8,128)(2,1)S(1)}, u32[]{:S(2)}, u32[]{:S(2)}) async-start(bf16[16,48,1536]{2,1,0:T(8,128)(2,1)} %bitcast.43), calls=%async_computation.1 | async-start | bytes 4718592 | tf_op jit(solution)/shard_map/all_to_all | solution.py:48
  268.9 0.2 lt.50
  269.1 0.1 copy.26
  269.1 0.0 copy-done.2
  269.2 0.1 copy.27
  269.3 114.2 %all-to-all-done.1 = bf16[16,48,1536]{2,1,0:T(8,128)(2,1)S(1)} async-done(((bf16[16,48,1536]{2,1,0:T(8,128)(2,1)}), bf16[16,48,1536]{2,1,0:T(8,128)(2,1)S(1)}, u32[]{:S(2)}, u32[]{:S(2)}) %all-to-all-start.1) | async-done | bytes 2359328 | tf_op jit(solution)/shard_map/all_to_all | solution.py:48
  383.6 3.9 gather_fusion.1
  387.4 5.0 %reshape.148 = f32[128,6,1536]{2,1,0:T(8,128)} reshape(bf16[768,1536]{1,0:T(8,128)(2,1)} %gather_fusion.1) | data formatting | bytes 7077888 | tf_op jit(solution)/shard_map/convert_element_type | solution.py:54
  392.4 5.9 %multiply_reduce_fusion = bf16[128,1536]{1,0:T(8,128)(2,1)} fusion(f32[128,6,1536]{2,1,0:T(8,128)} %reshape.148, f32[128,6]{1,0:T(8,128)S(1)} %copy.27), kind=kLoop, calls=%fused_computation.6 | loop fusion | flops 2162688 | bytes 5114880 | tf_op jit(solution)/shard_map/reduce_sum | solution.py:53
  (12 shorter events, 0.2 us)
Async XLA Ops:
  6.5 15.0 %copy-start = (bf16[128,1536]{1,0:T(8,128)(2,1)S(1)}, bf16[128,1536]{1,0:T(8,128)(2,1)}, u32[]{:S(2)}) copy-start(bf16[128,1536]{1,0:T(8,128)(2,1)} %param.7) | copy-start | bytes 1179652
  6.5 174.3 %all-gather.3.cloned.1.call-start = ((), (), s32[]{:S(2)}) async-start(), calls=%async_computation.2 | async-start | bytes 6488064 | tf_op jit(solution)/shard_map/all_gather | solution.py:37
  26.1 16.9 %copy-start.1 = (f32[2,512,48]{1,2,0:T(8,128)S(1)}, f32[2,512,48]{1,2,0:T(8,128)}, u32[]{:S(2)}) copy-start(f32[2,512,48]{1,2,0:T(8,128)} %param.10) | copy-start | bytes 589828
  26.1 122.5 %all-to-all-start = ((bf16[16,48,1536]{2,1,0:T(8,128)(2,1)}), bf16[16,48,1536]{2,1,0:T(8,128)(2,1)S(1)}, u32[]{:S(2)}, u32[]{:S(2)}) async-start(bf16[16,48,1536]{2,1,0:T(8,128)(2,1)} %broadcast_select_fusion), calls=%async_computation | async-start | bytes 4718592 | tf_op jit(solution)/shard_map/all_to_all | solution.py:32
  43.0 206.8 %all-gather.5.cloned.1.call-start = ((), (), s32[]{:S(2)}) async-start(), calls=%async_computation.3 | async-start | bytes 3244032 | tf_op jit(solution)/shard_map/all_gather | solution.py:38
  255.9 13.3 %copy-start.2 = (f32[128,6]{0,1:T(8,128)S(1)}, f32[128,6]{0,1:T(8,128)}, u32[]{:S(2)}) copy-start(f32[128,6]{0,1:T(8,128)} %param.12) | copy-start | bytes 9220
  255.9 127.7 %all-to-all-start.1 = ((bf16[16,48,1536]{2,1,0:T(8,128)(2,1)}), bf16[16,48,1536]{2,1,0:T(8,128)(2,1)S(1)}, u32[]{:S(2)}, u32[]{:S(2)}) async-start(bf16[16,48,1536]{2,1,0:T(8,128)(2,1)} %bitcast.43), calls=%async_computation.1 | async-start | bytes 4718592 | tf_op jit(solution)/shard_map/all_to_all | solution.py:48
Sparse Core Ops, SparseCore 0:
  9.4 171.3 all-gather.2
  182.9 66.8 all-gather.4
where the time goes:
time: 406 us; the launch traced here: 405 us
  waiting for transfers between devices  313 us (77%)
  starting transfers between devices  29.9 us (7%)
  local copies, waits for them, and re-layouts  22.8 us (6%)
  other arithmetic  14.2 us (3%)
  between operations  13.6 us (3%)
  matrix products  11.3 us (3%)
    all_to_all x1, waiting for transfers between devices, local(): lax.all_to_all(expert_rows, 'expert', split_axis=0, concat_axis=0, tiled=...  114 us
    all_to_all x1, waiting for transfers between devices, local(): lax.all_to_all(outgoing, 'expert', split_axis=0, concat_axis=0, tiled=True)  105 us
    all_gather x1, waiting for transfers between devices, local(): lax.all_gather(down_local, 'group', axis=2, tiled=True)  62 us
    all_gather x1, waiting for transfers between devices, local(): lax.all_gather(gate_up_local, 'group', axis=1, tiled=True)  32.2 us
    all_to_all x1, starting transfers between devices, local(): lax.all_to_all(outgoing, 'expert', split_axis=0, concat_axis=0, tiled=True)  16.9 us
    all_to_all x1, starting transfers between devices, local(): lax.all_to_all(expert_rows, 'expert', split_axis=0, concat_axis=0, tiled=...  13 us
  transfers between devices with their start and end apart: 4, of which 4 were waited for; matrix products, arithmetic and copies ran while one was open for 6% of the time, Pallas kernels for 0%

commit v1 on v0

--- a/solution.py
+++ b/solution.py
@@ -34,7 +34,10 @@
     gate_up_local = jnp.concatenate([gate_train, up_train], axis=2).astype(jnp.bfloat16)
     down_local = down_train.astype(jnp.bfloat16)
     gate_up_w, down_w = (
-        lax.all_gather(gate_up_local, "group", axis=1, tiled=True),
+        jnp.concatenate(
+            lax.all_to_all(jnp.stack([gate_up_local] * lax.axis_size("group")), "group", 0, 0),
+            axis=1,
+        ),
         lax.all_gather(down_local, "group", axis=2, tiled=True),
     )
     gate_up = jnp.einsum("sjcd,jdf->sjcf", incoming, gate_up_w, preferred_element_type=jnp.float32)

time: 406 us -> 478 us (1.18)
  the two profiles are of different devices: /device:TPU:48 before, /device:TPU:56 now
where the time goes in v1:
time: 478 us; the launch traced here: 477 us
  waiting for transfers between devices  370 us (77%)
  starting transfers between devices  38.4 us (8%)
  local copies, waits for them, and re-layouts  32.3 us (7%)
  between operations  13.6 us (3%)
  other arithmetic  12.1 us (3%)
  matrix products  11.4 us (2%)
    all_to_all x1, waiting for transfers between devices, local(): lax.all_to_all(jnp.stack([gate_up_local] * lax.axis_size('group')), 'grou...  121 us
    all_to_all x1, waiting for transfers between devices, local(): lax.all_to_all(expert_rows, 'expert', split_axis=0, concat_axis=0, tiled=...  120 us
    all_to_all x1, waiting for transfers between devices, local(): lax.all_to_all(outgoing, 'expert', split_axis=0, concat_axis=0, tiled=True)  107 us
    all_gather x1, waiting for transfers between devices, local(): lax.all_gather(down_local, 'group', axis=2, tiled=True)  23 us
    all_to_all x1, starting transfers between devices, local(): lax.all_to_all(expert_rows, 'expert', split_axis=0, concat_axis=0, tiled=...  14.7 us
    all_to_all x1, starting transfers between devices, local(): lax.all_to_all(outgoing, 'expert', split_axis=0, concat_axis=0, tiled=True)  13.8 us
    all_to_all x1, starting transfers between devices, local(): lax.all_to_all(jnp.stack([gate_up_local] * lax.axis_size('group')), 'grou...  9.9 us
  transfers between devices with their start and end apart: 4, of which 4 were waited for; matrix products, arithmetic and copies ran while one was open for 6% of the time, Pallas kernels for 0%

profile of v1, /device:TPU:56, one launch (start us, length us, event | category | flops | bytes accessed | tf_op | source)
XLA Modules:
  0.0 477.5 jit_solution(17292416520306783433)
XLA Ops:
  6.5 0.0 copy-start
  6.5 1.0 convert.7
  7.5 0.9 convert.8
  8.5 3.5 stack.2
  12.0 0.0 copy-start.4
  12.0 0.0 copy-start.2
  12.0 9.9 %all-to-all-start = ((bf16[32,2,48,1024]{3,2,1,0:T(8,128)(2,1)}), bf16[32,2,48,1024]{3,2,1,0:T(8,128)(2,1)}, u32[]{:S(2)}, u32[]{:S(2)}) async-start(bf16[32,2,48,1024]{3,2,1,0:T(8,128)(2,1)} %stack.2), calls=%async_computation | async-start | bytes 12582912 | tf_op jit(solution)/shard_map/all_to_all | solution.py:38
  21.9 0.0 copy-done.4
  21.9 0.1 broadcast_in_dim.37.clone
  22.0 0.2 gt.41
  22.1 0.1 gt.40
  22.3 0.0 copy-done.2
  22.3 0.1 copy.28
  22.4 0.1 eq.29
  22.5 0.1 eq.25
  22.7 0.1 gt.39
  22.9 1.7 reduce-window.6
  24.6 0.3 slice_reduce_fusion
  24.9 0.1 copy.33
  25.0 0.1 mul.37
  25.2 0.1 fusion.14
  25.3 3.4 scatter_custom_fusion.1
  28.7 3.4 scatter_custom_fusion
  32.1 0.1 broadcast_in_dim.40
  32.2 0.0 copy-done
  32.2 2.9 gather_fusion
  35.2 1.6 broadcast_select_fusion
  36.8 0.0 copy-start.1
  36.8 120.6 %all-to-all-done = bf16[32,2,48,1024]{3,2,1,0:T(8,128)(2,1)} async-done(((bf16[32,2,48,1024]{3,2,1,0:T(8,128)(2,1)}), bf16[32,2,48,1024]{3,2,1,0:T(8,128)(2,1)}, u32[]{:S(2)}, u32[]{:S(2)}) %all-to-all-start) | async-done | bytes 6291488 | tf_op jit(solution)/shard_map/all_to_all | solution.py:38
  157.4 13.8 %all-to-all-start.1 = ((bf16[16,48,1536]{2,1,0:T(8,128)(2,1)}), bf16[16,48,1536]{2,1,0:T(8,128)(2,1)S(1)}, u32[]{:S(2)}, u32[]{:S(2)}) async-start(bf16[16,48,1536]{2,1,0:T(8,128)(2,1)} %broadcast_select_fusion), calls=%async_computation.1 | async-start | bytes 4718592 | tf_op jit(solution)/shard_map/all_to_all | solution.py:32
  171.2 0.0 all-gather.2.cloned.1.call-start
  171.2 0.0 copy-done.1
  171.2 0.7 convert_element_type.34
  171.9 0.0 all-gather.2.cloned.1.call-update
  171.9 6.7 %copy.26 = bf16[2,32,48,1024]{3,2,1,0:T(8,128)(2,1)} copy(bf16[2,32,48,1024]{3,2,0,1:T(8,128)(2,1)} %bitcast) | data formatting | bytes 12582912 | tf_op jit(solution)/shard_map/reshape | solution.py:37
  178.6 106.6 %all-to-all-done.1 = bf16[16,48,1536]{2,1,0:T(8,128)(2,1)S(1)} async-done(((bf16[16,48,1536]{2,1,0:T(8,128)(2,1)}), bf16[16,48,1536]{2,1,0:T(8,128)(2,1)S(1)}, u32[]{:S(2)}, u32[]{:S(2)}) %all-to-all-start.1) | async-done | bytes 2359328 | tf_op jit(solution)/shard_map/all_to_all | solution.py:32
  285.2 7.0 %fusion.6 = f32[16,2,24,1024]{3,2,0,1:T(8,128)} fusion(bf16[2,1536,1024,1]{2,1,3,0:T(8,128)(2,1)} %bitcast.45, bf16[16,2,24,1536]{3,2,1,0:T(8,128)(2,1)S(1)} %bitcast.46), kind=kOutput, calls=%fused_computation.11 | convolution fusion | flops 2415919104 | bytes 11796480 | tf_op jit(solution)/shard_map/sjcd,jdf->sjcf/dot_general | solution.py:43
  292.3 23.0 %all-gather.2.cloned.1.call-done = bf16[2,512,1536]{1,2,0:T(8,128)(2,1)} async-done(((bf16[2,512,48]{1,2,0:T(8,128)(2,1)}), bf16[2,512,1536]{1,2,0:T(8,128)(2,1)}) %all-gather.2.cloned.1.call-update) | async-done | bytes 3145744 | tf_op jit(solution)/shard_map/all_gather | solution.py:41
  315.2 4.3 fusion.1
  319.6 1.7 copy.35
  321.3 0.0 copy-start.3
  321.3 14.7 %all-to-all-start.2 = ((bf16[16,48,1536]{2,1,0:T(8,128)(2,1)}), bf16[16,48,1536]{2,1,0:T(8,128)(2,1)S(1)}, u32[]{:S(2)}, u32[]{:S(2)}) async-start(bf16[16,48,1536]{2,1,0:T(8,128)(2,1)} %bitcast.43), calls=%async_computation.2 | async-start | bytes 4718592 | tf_op jit(solution)/shard_map/all_to_all | solution.py:51
  335.9 0.2 lt.50
  336.1 0.1 copy.36
  336.2 0.0 copy-done.3
  336.2 0.1 copy.37
  336.4 119.5 %all-to-all-done.2 = bf16[16,48,1536]{2,1,0:T(8,128)(2,1)S(1)} async-done(((bf16[16,48,1536]{2,1,0:T(8,128)(2,1)}), bf16[16,48,1536]{2,1,0:T(8,128)(2,1)S(1)}, u32[]{:S(2)}, u32[]{:S(2)}) %all-to-all-start.2) | async-done | bytes 2359328 | tf_op jit(solution)/shard_map/all_to_all | solution.py:51
  455.9 3.9 gather_fusion.1
  459.8 5.0 %reshape.163 = f32[128,6,1536]{2,1,0:T(8,128)} reshape(bf16[768,1536]{1,0:T(8,128)(2,1)} %gather_fusion.1) | data formatting | bytes 7077888 | tf_op jit(solution)/shard_map/convert_element_type | solution.py:57
  464.7 5.9 %multiply_reduce_fusion = bf16[128,1536]{1,0:T(8,128)(2,1)} fusion(f32[128,6,1536]{2,1,0:T(8,128)} %reshape.163, f32[128,6]{1,0:T(8,128)S(1)} %copy.37), kind=kLoop, calls=%fused_computation.4 | loop fusion | flops 2162688 | bytes 5114880 | tf_op jit(solution)/shard_map/reduce_sum | solution.py:56
  (15 shorter events, 0.2 us)
Async XLA Ops:
  6.5 25.7 %copy-start = (bf16[128,1536]{1,0:T(8,128)(2,1)S(1)}, bf16[128,1536]{1,0:T(8,128)(2,1)}, u32[]{:S(2)}) copy-start(bf16[128,1536]{1,0:T(8,128)(2,1)} %param.7) | copy-start | bytes 1179652
  12.0 9.9 %copy-start.4 = (s32[128]{0:T(128)S(1)}, s32[128]{0:T(128)}, u32[]{:S(2)}) copy-start(s32[128]{0:T(128)} %param.13) | copy-start | bytes 1540
  12.0 10.3 %copy-start.2 = (s32[128,6]{0,1:T(8,128)S(1)}, s32[128,6]{0,1:T(8,128)}, u32[]{:S(2)}) copy-start(s32[128,6]{0,1:T(8,128)} %param.11) | copy-start | bytes 9220
  12.0 145.4 %all-to-all-start = ((bf16[32,2,48,1024]{3,2,1,0:T(8,128)(2,1)}), bf16[32,2,48,1024]{3,2,1,0:T(8,128)(2,1)}, u32[]{:S(2)}, u32[]{:S(2)}) async-start(bf16[32,2,48,1024]{3,2,1,0:T(8,128)(2,1)} %stack.2), calls=%async_computation | async-start | bytes 12582912 | tf_op jit(solution)/shard_map/all_to_all | solution.py:38
  36.8 134.4 %copy-start.1 = (f32[2,512,48]{1,2,0:T(8,128)S(1)}, f32[2,512,48]{1,2,0:T(8,128)}, u32[]{:S(2)}) copy-start(f32[2,512,48]{1,2,0:T(8,128)} %param.10) | copy-start | bytes 589828
  157.4 127.8 %all-to-all-start.1 = ((bf16[16,48,1536]{2,1,0:T(8,128)(2,1)}), bf16[16,48,1536]{2,1,0:T(8,128)(2,1)S(1)}, u32[]{:S(2)}, u32[]{:S(2)}) async-start(bf16[16,48,1536]{2,1,0:T(8,128)(2,1)} %broadcast_select_fusion), calls=%async_computation.1 | async-start | bytes 4718592 | tf_op jit(solution)/shard_map/all_to_all | solution.py:32
  171.2 144.1 %all-gather.2.cloned.1.call-start = ((), (), s32[]{:S(2)}) async-start(), calls=%async_computation.3 | async-start | bytes 3244032 | tf_op jit(solution)/shard_map/all_gather | solution.py:41
  321.3 14.9 %copy-start.3 = (f32[128,6]{0,1:T(8,128)S(1)}, f32[128,6]{0,1:T(8,128)}, u32[]{:S(2)}) copy-start(f32[128,6]{0,1:T(8,128)} %param.12) | copy-start | bytes 9220
  321.3 134.6 %all-to-all-start.2 = ((bf16[16,48,1536]{2,1,0:T(8,128)(2,1)}), bf16[16,48,1536]{2,1,0:T(8,128)(2,1)S(1)}, u32[]{:S(2)}, u32[]{:S(2)}) async-start(bf16[16,48,1536]{2,1,0:T(8,128)(2,1)} %bitcast.43), calls=%async_computation.2 | async-start | bytes 4718592 | tf_op jit(solution)/shard_map/all_to_all | solution.py:51
Sparse Core Ops, SparseCore 0:
  174.1 141.1 all-gather.1
